TPU v7x, 32 devices: a whole 2x2x4 slice. The times are simulated.
32 devices in a mesh: grp: 2 (over x), lat: 16 (over z, y, core).
Axes of the slice: x: 2, y: 2, z: 4, core: 2. Of those that a mesh axis runs over, the one named last changes fastest.
Arguments:
- activations: bfloat16 [64, 1440, 384], P(('grp', 'lat')), parts along dimension 0, may hold values from -6 to 6
- upstream: bfloat16 [64, 1440, 384], P(('grp', 'lat')), parts along dimension 0, may hold values from -6 to 6
- skip_weight: bfloat16 [384, 384], replicated, may hold values from -0.3125 to 0.3125
- spectral_weight: bfloat16 [32, 2, 384, 384], P('lat'), may hold values from -2.5 to 2.5
- slot_degree: int32 [32], replicated, may hold values from 0 to 31, each once
Outputs:
- grad_activations: bfloat16 [64, 1440, 384], P(('grp', 'lat')), parts along dimension 0
- grad_spectral: bfloat16 [64, 2, 384, 384], P(('grp', 'lat')), parts along dimension 0
- grad_skip: float32 [768, 384], P(('grp', 'lat')), parts along dimension 0
There are 2 independent parts, one for each index of `grp`. A program takes and returns all parts, laid end to end along the dimension named above; an argument that names none is the same for every part. Nothing has to cross between parts.
Inputs may be any that keep to these rules, and one draw needn't show every extreme that they name: `slot_degree`: device d holds slots d * 2 to (d + 1) * 2 - 1 of spectral_weight and grad_spectral; every degree appears in exactly one slot.
All inputs are finite; a program needn't handle non-finite values.
Results may differ from a plain program's by a relative error of at most 0.013.
Values may be sent and summed in bfloat16 or wider, within the bound.
No kernel may reach another device: no remote copies, remote signals or barrier semaphores. Data moves between devices by JAX's collectives and lax.ppermute only.
A program may use at most 64 MiB of HBM per device.

v0:
```python
import math
import jax
import jax.numpy as jnp
from jax import lax
from jax.sharding import PartitionSpec as P

ORDERS = 4
highest = lax.Precision.HIGHEST


def fourier_table(lon_total, orders):
    lon_ids = jnp.arange(lon_total, dtype=jnp.int32)[:, None]
    order_ids = jnp.arange(orders, dtype=jnp.int32)[None, :]
    angles = (lon_ids * order_ids % lon_total).astype(jnp.float32) * (2.0 * math.pi / lon_total)
    amplitude = math.sqrt(2.0 / lon_total)
    return jnp.concatenate(
        [amplitude * jnp.cos(angles), -amplitude * jnp.sin(angles)], axis=1
    ).astype(jnp.bfloat16)


def colatitudes(row_ids, lat_total):
    mirror = jnp.minimum(row_ids, lat_total - 1 - row_ids)
    colatitude = (mirror.astype(jnp.float32) + 0.5) * (math.pi / lat_total)
    cosines = jnp.where(row_ids < lat_total // 2, jnp.cos(colatitude), -jnp.cos(colatitude))
    return (cosines, jnp.sin(colatitude))


def legendre_table(cosines, sines, degrees, orders):
    order_col = jnp.arange(orders, dtype=jnp.float32)[:, None]
    factors = [math.sqrt(0.5)]
    for order_num in range(1, orders):
        factors.append(factors[-1] * math.sqrt((2.0 * order_num + 1.0) / (2.0 * order_num)))
    diagonal_start = jnp.array(factors, dtype=jnp.float32)[:, None] * jnp.power(
        sines[None, :], order_col
    )
    next_start = jnp.sqrt(2.0 * order_col + 3.0) * cosines[None, :] * diagonal_start

    def advance(state_pair, degree):
        previous, earlier = state_pair
        deg_value = degree.astype(jnp.float32)
        deg_below = deg_value - 1.0
        ratio_up = jnp.sqrt(
            jnp.maximum(4.0 * deg_value * deg_value - 1.0, 1.0)
            / jnp.maximum(deg_value * deg_value - order_col * order_col, 1.0)
        )
        ratio_down = jnp.sqrt(
            jnp.maximum(deg_below * deg_below - order_col * order_col, 0.0)
            / jnp.maximum(4.0 * deg_below * deg_below - 1.0, 1.0)
        )
        recurred = ratio_up * (cosines[None, :] * previous - ratio_down * earlier)
        current = jnp.where(
            deg_value == order_col,
            diagonal_start,
            jnp.where(
                deg_value == order_col + 1.0,
                next_start,
                jnp.where(deg_value > order_col + 1.0, recurred, 0.0),
            ),
        )
        return ((current, previous), current)

    zeroed = jnp.zeros((orders, cosines.shape[0]), jnp.float32)
    _, stacked = lax.scan(advance, (zeroed, zeroed), jnp.arange(degrees, dtype=jnp.int32))
    return jnp.concatenate([stacked, stacked], axis=1)


def gelu_tanh(values):
    return jax.nn.gelu(values, approximate=True)


def complex_apply(coeffs, weights, orders):
    real_in, imag_in = (coeffs[:, :orders], coeffs[:, orders:])
    real_w, imag_w = (weights[:, 0], weights[:, 1])

    def complex_term(operand_a, operand_b):
        return jnp.einsum("smc,scd->smd", operand_a, operand_b, preferred_element_type=jnp.float32)

    real_out = complex_term(real_in, real_w) - complex_term(imag_in, imag_w)
    imag_out = complex_term(real_in, imag_w) + complex_term(imag_in, real_w)
    return jnp.concatenate([real_out, imag_out], axis=1)


def complex_adjoint(coeffs, cotangents, weights, orders):
    real_in, imag_in = (coeffs[:, :orders], coeffs[:, orders:])
    real_g, imag_g = (cotangents[:, :orders], cotangents[:, orders:])
    real_w, imag_w = (weights[:, 0], weights[:, 1])

    def outer_sum(operand_a, operand_b):
        return jnp.einsum("smc,smd->scd", operand_a, operand_b, preferred_element_type=jnp.float32)

    def back_term(operand_a, operand_b):
        return jnp.einsum("smd,scd->smc", operand_a, operand_b, preferred_element_type=jnp.float32)

    grad_real = outer_sum(real_in, real_g) + outer_sum(imag_in, imag_g)
    grad_imag = outer_sum(real_in, imag_g) - outer_sum(imag_in, real_g)
    back_real = back_term(real_g, real_w) + back_term(imag_g, imag_w)
    back_imag = back_term(imag_g, real_w) - back_term(real_g, imag_w)
    return (
        jnp.stack([grad_real, grad_imag], axis=1),
        jnp.concatenate([back_real, back_imag], axis=1),
    )


def local(activations, upstream, skip_weight, spectral_weight, slot_degree):
    groups = lax.axis_size("lat")
    lat_rows = activations.shape[0]
    lon_total = activations.shape[1]
    lat_total = lat_rows * groups
    per_owner = spectral_weight.shape[0]
    degrees = per_owner * groups
    orders = ORDERS
    fourier = fourier_table(lon_total, orders)
    spectrum = jnp.einsum("jkc,kf->jfc", activations, fourier, preferred_element_type=jnp.float32)
    all_rows = jnp.arange(lat_total, dtype=jnp.int32)
    cos_all, sin_all = colatitudes(all_rows, lat_total)
    slot_plm = jnp.take(legendre_table(cos_all, sin_all, degrees, orders), slot_degree, axis=0)
    slot_quad = slot_plm * (math.pi / lat_total * sin_all)[None, None, :]

    def to_channels(values):
        return lax.all_to_all(values, "lat", split_axis=2, concat_axis=0, tiled=True)

    def to_owners(values):
        return lax.all_to_all(values, "lat", split_axis=0, concat_axis=2, tiled=True)

    def from_owners(values):
        return lax.all_to_all(values, "lat", split_axis=2, concat_axis=0, tiled=True)

    def to_rows(values):
        return lax.all_to_all(values, "lat", split_axis=0, concat_axis=2, tiled=True)

    by_channel = to_channels(spectrum)
    coeffs = to_owners(
        jnp.einsum("sfj,jfc->sfc", slot_quad, by_channel, precision=highest).astype(jnp.bfloat16)
    )
    filtered = complex_apply(coeffs, spectral_weight, orders).astype(jnp.bfloat16)
    spread = from_owners(filtered).astype(jnp.float32)
    grid_modes = to_rows(
        jnp.einsum("sfj,sfc->jfc", slot_plm, spread, precision=highest).astype(jnp.bfloat16)
    )
    spatial = jnp.einsum("jfc,kf->jkc", grid_modes, fourier, preferred_element_type=jnp.float32)
    skip_out = jnp.einsum(
        "jkc,cd->jkd", activations, skip_weight, preferred_element_type=jnp.float32
    )
    _, pullback = jax.vjp(gelu_tanh, spatial + skip_out)
    slope_b = pullback(upstream.astype(jnp.float32))[0].astype(jnp.bfloat16)
    grad_skip = lax.psum_scatter(
        jnp.einsum("jkc,jkd->cd", activations, slope_b, preferred_element_type=jnp.float32),
        "lat",
        scatter_dimension=0,
        tiled=True,
    ) * (1.0 / math.sqrt(lat_total * lon_total))
    through_skip = jnp.einsum(
        "jkd,cd->jkc", slope_b, skip_weight, preferred_element_type=jnp.float32
    )
    mode_grads = jnp.einsum("jkc,kf->jfc", slope_b, fourier, preferred_element_type=jnp.float32)
    grads_by_channel = to_channels(mode_grads)
    coeff_grads = to_owners(
        jnp.einsum("sfj,jfc->sfc", slot_plm, grads_by_channel, precision=highest).astype(
            jnp.bfloat16
        )
    )
    weight_grads, back_coeffs = complex_adjoint(coeffs, coeff_grads, spectral_weight, orders)
    back_b = back_coeffs.astype(jnp.bfloat16)
    back_spread = from_owners(back_b).astype(jnp.float32)
    row_grads = to_rows(
        jnp.einsum("sfj,sfc->jfc", slot_quad, back_spread, precision=highest).astype(jnp.bfloat16)
    )
    through_modes = jnp.einsum(
        "jfc,kf->jkc", row_grads, fourier, preferred_element_type=jnp.float32
    )
    grad_activations = (upstream.astype(jnp.float32) + through_skip + through_modes).astype(
        jnp.bfloat16
    )
    return (grad_activations, weight_grads.astype(jnp.bfloat16), grad_skip)


def solution(mesh):
    in_specs = (
        P(("grp", "lat"), None, None),
        P(("grp", "lat"), None, None),
        P(),
        P("lat", None, None, None),
        P(),
    )
    out_specs = (
        P(("grp", "lat"), None, None),
        P(("grp", "lat"), None, None, None),
        P(("grp", "lat"), None),
    )
    return jax.shard_map(local, mesh=mesh, in_specs=in_specs, out_specs=out_specs, check_vma=False)
```

profile of v0, /device:TPU:0, one launch (start us, length us, event | category | flops | bytes accessed | tf_op | source)
XLA Modules:
  0.0 300.9 jit_solution(992449923088837298)
XLA Ops:
  10.1 2.2 reshape.143
  12.3 7.4 %all-to-all-start = ((f32[16,1,384]{2,1,0:T(1,128)}), f32[16,1,384]{2,1,0:T(1,128)}, u32[]{:S(2)}, u32[]{:S(2)}) async-start(f32[16,1,384]{2,1,0:T(1,128)} %reshape.143), calls=%async_computation | async-start | bytes 49152 | tf_op jit(solution)/shard_map/all_to_all | solution.py:120
  20.0 67.6 %while.21 = (s32[]{:T(128)}, f32[4,32]{1,0:T(4,128)S(1)}, f32[4,32]{1,0:T(4,128)S(1)}, f32[32,4,32]{2,1,0:T(4,128)}, s32[32]{0:T(128)S(1)}, /*index=5*/f32[32]{0...) while((s32[]{:T(128)}, f32[4,32]{1,0:T(4,128)S(1)}, ...), condition=%wide.region_1.2_spmd.clone.clone.clone.clone, body=%wide.region_0.1_spmd.clone.clone.clone.clone.sunk | while | flops 1723 | bytes 5059 | solution.py:63
  93.9 2.1 reshape.144
  102.8 12.4 %all_to_all.144 = bf16[16,2,192]{2,1,0:T(2,128)(2,1)} all-to-all(bf16[16,2,192]{2,1,0:T(2,128)(2,1)} %reshape.145), channel_id=1, replica_groups=mesh['grp'=2,'lat'=16] {'lat'}, dimensions={0} | all-to-all | bytes 24576 | tf_op jit(solution)/shard_map/all_to_all | solution.py:123
  123.9 10.5 %all_to_all.145 = bf16[16,2,192]{2,1,0:T(2,128)(2,1)} all-to-all(bf16[16,2,192]{2,1,0:T(2,128)(2,1)} %reshape.147), channel_id=1, replica_groups=mesh['grp'=2,'lat'=16] {'lat'}, dimensions={0} | all-to-all | bytes 24576 | tf_op jit(solution)/shard_map/all_to_all | solution.py:126
  142.6 10.5 %all_to_all.146 = bf16[16,2,192]{2,1,0:T(2,128)(2,1)} all-to-all(bf16[16,2,192]{2,1,0:T(2,128)(2,1)} %reshape.149), channel_id=1, replica_groups=mesh['grp'=2,'lat'=16] {'lat'}, dimensions={0} | all-to-all | bytes 24576 | tf_op jit(solution)/shard_map/all_to_all | solution.py:129
  159.2 4.4 %fusion.33 = bf16[2,1440,384]{2,1,0:T(8,128)(2,1)S(1)} fusion(bf16[2,1440,384]{2,1,0:T(8,128)(2,1)S(1)} %copy-done.5, f32[1440,2,384]{2,0,1:T(8,128)S(1)} %fusion.109, bf16[2,1440,384]{2,1,0:T(8,128)(2,1)S(1)} %copy-done, bf16[384,384]{1,0:T(8,128)(2,1)S(1)} %copy-done.12), kind=kOutput, calls=%fused_computation.45 | convolution fusion | flops 873676800 | bytes 11354112 | tf_op jit(solution)/shard_map/jkc,cd->jkd/dot_general | solution.py:141
  167.7 2.2 reshape.151
  169.9 4.1 %all-to-all-start.4 = ((f32[16,1,384]{2,1,0:T(1,128)}), f32[16,1,384]{2,1,0:T(1,128)}, u32[]{:S(2)}, u32[]{:S(2)}) async-start(f32[16,1,384]{2,1,0:T(1,128)} %reshape.151), calls=%async_computation.4 | async-start | bytes 49152 | tf_op jit(solution)/shard_map/all_to_all | solution.py:120
  175.3 5.3 %all-to-all-done.4 = f32[16,1,384]{2,1,0:T(1,128)} async-done(((f32[16,1,384]{2,1,0:T(1,128)}), f32[16,1,384]{2,1,0:T(1,128)}, u32[]{:S(2)}, u32[]{:S(2)}) %all-to-all-start.4) | async-done | bytes 24608 | tf_op jit(solution)/shard_map/all_to_all | solution.py:120
  180.6 2.0 reduce.1
  182.6 2.1 reshape.152
  186.5 2.0 fusion.45
  191.6 3.5 %all-to-all-start.5 = ((bf16[16,2,192]{2,1,0:T(2,128)(2,1)}), bf16[16,2,192]{2,1,0:T(2,128)(2,1)S(1)}, u32[]{:S(2)}, u32[]{:S(2)}) async-start(bf16[16,2,192]{2,1,0:T(2,128)(2,1)} %reshape.153), calls=%async_computation.5 | async-start | bytes 32768 | tf_op jit(solution)/shard_map/all_to_all | solution.py:123
  195.3 3.8 %convolution_bitcast_fusion = f32[384,384]{0,1:T(8,128)} fusion(bf16[2,1440,384]{2,1,0:T(8,128)(2,1)} %copy-done.1, bf16[2,1440,384]{2,1,0:T(8,128)(2,1)S(1)} %copy-done), kind=kOutput, calls=%fused_computation.56 | convolution fusion | flops 849346560 | bytes 5013504 | tf_op jit(solution)/shard_map/jkc,jkd->cd/dot_general | solution.py:147
  199.2 2.4 all-to-all-done.5
  212.6 4.1 %all-to-all-start.6 = ((bf16[16,2,192]{2,1,0:T(2,128)(2,1)}), bf16[16,2,192]{2,1,0:T(2,128)(2,1)}, u32[]{:S(2)}, u32[]{:S(2)}) async-start(bf16[16,2,192]{2,1,0:T(2,128)(2,1)} %reshape.155), calls=%async_computation.6 | async-start | bytes 32768 | tf_op jit(solution)/shard_map/all_to_all | solution.py:126
  216.6 2.5 fusion.41
  220.3 2.9 all-to-all-done.6
  225.4 3.5 %all-to-all-start.7 = ((bf16[16,2,192]{2,1,0:T(2,128)(2,1)}), bf16[16,2,192]{2,1,0:T(2,128)(2,1)S(1)}, u32[]{:S(2)}, u32[]{:S(2)}) async-start(bf16[16,2,192]{2,1,0:T(2,128)(2,1)} %reshape.157), calls=%async_computation.7 | async-start | bytes 32768 | tf_op jit(solution)/shard_map/all_to_all | solution.py:129
  231.5 3.9 %all-to-all-done.7 = bf16[16,2,192]{2,1,0:T(2,128)(2,1)S(1)} async-done(((bf16[16,2,192]{2,1,0:T(2,128)(2,1)}), bf16[16,2,192]{2,1,0:T(2,128)(2,1)S(1)}, u32[]{:S(2)}, u32[]{:S(2)}) %all-to-all-start.7) | async-done | bytes 12320 | tf_op jit(solution)/shard_map/all_to_all | solution.py:129
  238.0 3.9 %fusion.38 = bf16[2,1440,384]{2,1,0:T(8,128)(2,1)} fusion(bf16[2,1440,384]{2,1,0:T(8,128)(2,1)S(1)} %copy-done.6, f32[1440,2,384]{2,0,1:T(8,128)S(1)} %fusion.108, bf16[2,1440,384]{2,1,0:T(8,128)(2,1)S(1)} %copy-done.2, bf16[384,384]{1,0:T(8,128)(2,1)} %param.10), kind=kOutput, calls=%fused_computation.50 | convolution fusion | flops 853770240 | bytes 11354112 | tf_op jit(solution)/shard_map/jkd,cd->jkc/dot_general | solution.py:152
  241.9 50.3 %all-reduce.3.cloned.1.call-done = f32[384,384]{0,1:T(8,128)} async-done(((f32[384,384]{0,1:T(8,128)}), f32[384,384]{0,1:T(8,128)}) %all-reduce.3.cloned.1.call-update) | async-done | bytes 589840
  (300 shorter events, 115.0 us)
Async XLA Ops:
  7.2 1.7 copy-start
  7.2 12.8 %copy-start.13 = (f32[4]{0:T(128)S(1)}, f32[4]{0:T(128)}, u32[]{:S(2)}) copy-start(f32[4]{0:T(128)} %constant.106.clone) | copy-start | bytes 52
  7.2 12.7 %copy-start.14 = (s32[32]{0:T(128)S(1)}, s32[32]{0:T(128)}, u32[]{:S(2)}) copy-start(s32[32]{0:T(128)} %param.12) | copy-start | bytes 388
  7.4 0.6 copy-start.9
  7.4 156.2 %copy-start.7 = (bf16[1440,4]{0,1:T(4,128)(2,1)}, bf16[1440,4]{0,1:T(4,128)(2,1)S(1)}, u32[]{:S(2)}) copy-start(bf16[1440,4]{0,1:T(4,128)(2,1)S(1)} %get-tuple-element.333) | copy-start | bytes 34564
  9.2 109.9 %copy-start.3 = (bf16[2,2,384,384]{3,2,1,0:T(8,128)(2,1)S(1)}, bf16[2,2,384,384]{3,2,1,0:T(8,128)(2,1)}, u32[]{:S(2)}) copy-start(bf16[2,2,384,384]{3,2,1,0:T(8,128)(2,1)} %param.11) | copy-start | bytes 3538948
  12.3 79.1 %all-to-all-start = ((f32[16,1,384]{2,1,0:T(1,128)}), f32[16,1,384]{2,1,0:T(1,128)}, u32[]{:S(2)}, u32[]{:S(2)}) async-start(f32[16,1,384]{2,1,0:T(1,128)} %reshape.143), calls=%async_computation | async-start | bytes 49152 | tf_op jit(solution)/shard_map/all_to_all | solution.py:120
  157.6 1.7 copy-start.5
  157.6 1.7 copy-start.12
  159.2 5.8 %copy-start.10 = (bf16[1440,4]{0,1:T(4,128)(2,1)S(1)}, bf16[1440,4]{0,1:T(4,128)(2,1)}, u32[]{:S(2)}) copy-start(bf16[1440,4]{0,1:T(4,128)(2,1)} %copy-done.9) | copy-start | bytes 34564
  163.7 1.4 copy-start.1
  165.0 9.0 %copy-start.15 = (u32[32]{0:T(128)S(1)}, u32[32]{0:T(128)}, u32[]{:S(2)}) copy-start(u32[32]{0:T(128)} %constant.112) | copy-start | bytes 388
  169.9 10.7 %all-to-all-start.4 = ((f32[16,1,384]{2,1,0:T(1,128)}), f32[16,1,384]{2,1,0:T(1,128)}, u32[]{:S(2)}, u32[]{:S(2)}) async-start(f32[16,1,384]{2,1,0:T(1,128)} %reshape.151), calls=%async_computation.4 | async-start | bytes 49152 | tf_op jit(solution)/shard_map/all_to_all | solution.py:120
  191.6 10.0 %all-to-all-start.5 = ((bf16[16,2,192]{2,1,0:T(2,128)(2,1)}), bf16[16,2,192]{2,1,0:T(2,128)(2,1)S(1)}, u32[]{:S(2)}, u32[]{:S(2)}) async-start(bf16[16,2,192]{2,1,0:T(2,128)(2,1)} %reshape.153), calls=%async_computation.5 | async-start | bytes 32768 | tf_op jit(solution)/shard_map/all_to_all | solution.py:123
  195.1 97.1 %all-reduce.3.cloned.1.call-start = ((), (), s32[]{:S(2)}) async-start(), calls=%async_computation.8 | async-start | bytes 1179648
  208.6 10.5 %copy-start.4 = (f32[2,384,384]{2,1,0:T(8,128)S(1)}, f32[2,384,384]{2,1,0:T(8,128)}, u32[]{:S(2)}) copy-start(f32[2,384,384]{2,1,0:T(8,128)} %fusion.92) | copy-start | bytes 3538948
  212.6 10.6 %all-to-all-start.6 = ((bf16[16,2,192]{2,1,0:T(2,128)(2,1)}), bf16[16,2,192]{2,1,0:T(2,128)(2,1)}, u32[]{:S(2)}, u32[]{:S(2)}) async-start(bf16[16,2,192]{2,1,0:T(2,128)(2,1)} %reshape.155), calls=%async_computation.6 | async-start | bytes 32768 | tf_op jit(solution)/shard_map/all_to_all | solution.py:126
  225.4 10.0 %all-to-all-start.7 = ((bf16[16,2,192]{2,1,0:T(2,128)(2,1)}), bf16[16,2,192]{2,1,0:T(2,128)(2,1)S(1)}, u32[]{:S(2)}, u32[]{:S(2)}) async-start(bf16[16,2,192]{2,1,0:T(2,128)(2,1)} %reshape.157), calls=%async_computation.7 | async-start | bytes 32768 | tf_op jit(solution)/shard_map/all_to_all | solution.py:129
  228.9 6.7 %copy-start.8 = (bf16[1440,4]{0,1:T(4,128)(2,1)S(1)}, bf16[1440,4]{0,1:T(4,128)(2,1)}, u32[]{:S(2)}) copy-start(bf16[1440,4]{0,1:T(4,128)(2,1)} %copy-done.7) | copy-start | bytes 34564
  228.9 6.7 %copy-start.11 = (bf16[1440,4]{0,1:T(4,128)(2,1)S(1)}, bf16[1440,4]{0,1:T(4,128)(2,1)}, u32[]{:S(2)}) copy-start(bf16[1440,4]{0,1:T(4,128)(2,1)} %copy-done.9) | copy-start | bytes 34564
  235.7 1.6 copy-start.2
  235.7 2.3 copy-start.6
Sparse Core Ops, SparseCore 0:
  199.3 92.8 all-reduce.2
where the time goes:
time: 303 us; the launch traced here: 301 us
  local copies, waits for them, and re-layouts  76.7 us (25%)
  waiting for transfers between devices  64.8 us (21%)
  other arithmetic  34.8 us (11%)
  blocking collectives  33.4 us (11%)
  matrix products  30.5 us (10%)
  starting transfers between devices  22.9 us (8%)
  loops' own time  22.8 us (8%)
  between operations  15 us (5%)
    unnamed x2, waiting for transfers between devices  50.3 us
    unnamed x51, local copies, waits for them, and re-layouts  30.5 us
    another operation x1, loops' own time, legendre_table(): lax.scan(advance, (zeroed, zeroed), jnp.arange(degrees, dtype=jnp.int32))  22.8 us
    dynamic_update_slice x32, other arithmetic, legendre_table(): lax.scan(advance, (zeroed, zeroed), jnp.arange(degrees, dtype=jnp.int32))  21.2 us
    dynamic_slice x32, local copies, waits for them, and re-layouts, legendre_table(): lax.scan(advance, (zeroed, zeroed), jnp.arange(degrees, dtype=jnp.int32))  20.7 us
    all_to_all x1, blocking collectives, to_owners(): lax.all_to_all(values, 'lat', split_axis=0, concat_axis=2, tiled=True)  12.4 us
    all_to_all x2, starting transfers between devices, to_channels(): lax.all_to_all(values, 'lat', split_axis=2, concat_axis=0, tiled=True)  11.6 us
    all_to_all x1, blocking collectives, from_owners(): lax.all_to_all(values, 'lat', split_axis=2, concat_axis=0, tiled=True)  10.5 us
  transfers between devices with their start and end apart: 6, of which 5 were waited for; matrix products, arithmetic and copies ran while one was open for 25% of the time, Pallas kernels for 0%

commit v1 on v0

--- a/solution.py
+++ b/solution.py
@@ -120,7 +120,16 @@
         return lax.all_to_all(values, "lat", split_axis=2, concat_axis=0, tiled=True)
 
     def to_owners(values):
-        return lax.all_to_all(values, "lat", split_axis=0, concat_axis=2, tiled=True)
+
+        def list_samples_all_in(field, mesh_name):
+            return jnp.concatenate(
+                lax.all_to_all(
+                    jnp.stack(jnp.split(field, lax.axis_size(mesh_name), axis=0)), mesh_name, 0, 0
+                ),
+                axis=2,
+            )
+
+        return list_samples_all_in(values, "lat")
 
     def from_owners(values):
         return lax.all_to_all(values, "lat", split_axis=2, concat_axis=0, tiled=True)

time: 303 us -> 353 us (1.17)
  local copies, waits for them, and re-layouts: 76.7 us -> 146 us
  other arithmetic: 34.8 us -> 14.6 us
    another operation x0 -> x36, local copies, waits for them, and re-layouts: none -> 44.6 us  [list_samples_all_in(): jnp.stack(jnp.split(field, lax.axis_size(mesh_name), axis=0))]
    unnamed x51 -> x81, local copies, waits for them, and re-layouts: 30.5 us -> 60.9 us
    dynamic_update_slice x32, other arithmetic: 21.2 us -> 2.69 us  [legendre_table(): lax.scan(advance, (zeroed, zeroed), jnp.arange(degrees, dtype=jnp.int32))]
    all_to_all x4 -> x0, local copies, waits for them, and re-layouts: 4.87 us -> none  [to_owners(): lax.all_to_all(values, 'lat', split_axis=0, concat_axis=2, tiled=True)]
    reshape x0 -> x4, local copies, waits for them, and re-layouts: none -> 4.87 us  [list_samples_all_in(): jnp.concatenate(lax.all_to_all(jnp.stack(jnp.split(field, lax.axis_size(m...]
  transfers between devices with their start and end apart: 6 -> 6, of which waited for: 5 -> 5; matrix products, arithmetic and copies ran while one was open for 25% -> 16% of each run, Pallas kernels for 0% -> 0%
where the time goes in v1:
time: 353 us; the launch traced here: 348 us
  local copies, waits for them, and re-layouts  146 us (41%)
  waiting for transfers between devices  65 us (18%)
  blocking collectives  33.8 us (10%)
  matrix products  29.2 us (8%)
  starting transfers between devices  22.9 us (6%)
  loops' own time  22 us (6%)
  between operations  15.1 us (4%)
  other arithmetic  14.6 us (4%)
    unnamed x81, local copies, waits for them, and re-layouts  60.9 us
    unnamed x2, waiting for transfers between devices  50.3 us
    another operation x36, local copies, waits for them, and re-layouts, list_samples_all_in(): jnp.stack(jnp.split(field, lax.axis_size(mesh_name), axis=0))  44.6 us
    another operation x1, loops' own time, legendre_table(): lax.scan(advance, (zeroed, zeroed), jnp.arange(degrees, dtype=jnp.int32))  22 us
    dynamic_slice x32, local copies, waits for them, and re-layouts, legendre_table(): lax.scan(advance, (zeroed, zeroed), jnp.arange(degrees, dtype=jnp.int32))  18.8 us
    all_to_all x1, blocking collectives, list_samples_all_in(): lax.all_to_all(jnp.stack(jnp.split(field, lax.axis_size(mesh_name), axis=...  12.6 us
    all_to_all x2, starting transfers between devices, to_channels(): lax.all_to_all(values, 'lat', split_axis=2, concat_axis=0, tiled=True)  11.6 us
    all_to_all x1, blocking collectives, from_owners(): lax.all_to_all(values, 'lat', split_axis=2, concat_axis=0, tiled=True)  10.6 us
  transfers between devices with their start and end apart: 6, of which 5 were waited for; matrix products, arithmetic and copies ran while one was open for 16% of the time, Pallas kernels for 0%

profile of v1, /device:TPU:0, one launch (start us, length us, event | category | flops | bytes accessed | tf_op | source)
XLA Modules:
  0.0 348.1 jit_solution(57159928229270359)
XLA Ops:
  10.6 7.4 %all-to-all-start = ((f32[16,1,384]{2,1,0:T(1,128)}), f32[16,1,384]{2,1,0:T(1,128)}, u32[]{:S(2)}, u32[]{:S(2)}) async-start(f32[16,1,384]{2,1,0:T(1,128)} %reshape.159), calls=%async_computation | async-start | bytes 49152 | tf_op jit(solution)/shard_map/all_to_all | solution.py:120
  18.2 46.4 %while.21 = (s32[]{:T(128)}, f32[4,32]{1,0:T(4,128)S(1)}, f32[4,32]{1,0:T(4,128)S(1)}, f32[32,4,32]{2,1,0:T(4,128)S(1)}, s32[32]{0:T(128)S(1)}, /*index=5*/f32[3...) while((s32[]{:T(128)}, f32[4,32]{1,0:T(4,128)S(1)}, ...), condition=%wide.region_1.2_spmd.clone.clone.clone.clone, body=%wide.region_0.1_spmd.clone.clone.clone.clone.sunk | while | flops 1723 | bytes 15863 | solution.py:63
  66.6 2.0 reduce
  68.6 2.1 reshape.160
  113.4 12.6 %all_to_all.118 = bf16[16,2,192]{2,1,0:T(2,128)(2,1)} all-to-all(bf16[16,2,192]{2,1,0:T(2,128)(2,1)} %reshape.161), channel_id=1, replica_groups=mesh['grp'=2,'lat'=16] {'lat'}, dimensions={0} | all-to-all | bytes 24576 | tf_op jit(solution)/shard_map/all_to_all | solution.py:126
  134.6 10.6 %all_to_all.119 = bf16[16,2,192]{2,1,0:T(2,128)(2,1)} all-to-all(bf16[16,2,192]{2,1,0:T(2,128)(2,1)} %reshape.163), channel_id=1, replica_groups=mesh['grp'=2,'lat'=16] {'lat'}, dimensions={0} | all-to-all | bytes 24576 | tf_op jit(solution)/shard_map/all_to_all | solution.py:135
  148.5 1.8 fusion.44
  153.5 10.6 %all_to_all.120 = bf16[16,2,192]{2,1,0:T(2,128)(2,1)} all-to-all(bf16[16,2,192]{2,1,0:T(2,128)(2,1)} %reshape.165), channel_id=1, replica_groups=mesh['grp'=2,'lat'=16] {'lat'}, dimensions={0} | all-to-all | bytes 24576 | tf_op jit(solution)/shard_map/all_to_all | solution.py:138
  170.3 4.4 %fusion.33 = bf16[2,1440,384]{2,1,0:T(8,128)(2,1)S(1)} fusion(bf16[2,1440,384]{2,1,0:T(8,128)(2,1)S(1)} %copy-done.5, f32[1440,2,384]{2,0,1:T(8,128)S(1)} %fusion.109, bf16[2,1440,384]{2,1,0:T(8,128)(2,1)S(1)} %copy-done, bf16[384,384]{1,0:T(8,128)(2,1)S(1)} %copy-done.12), kind=kOutput, calls=%fused_computation.45 | convolution fusion | flops 873676800 | bytes 11354112 | tf_op jit(solution)/shard_map/jkc,cd->jkd/dot_general | solution.py:150
  178.8 2.2 reshape.167
  180.9 4.1 %all-to-all-start.4 = ((f32[16,1,384]{2,1,0:T(1,128)}), f32[16,1,384]{2,1,0:T(1,128)}, u32[]{:S(2)}, u32[]{:S(2)}) async-start(f32[16,1,384]{2,1,0:T(1,128)} %reshape.167), calls=%async_computation.4 | async-start | bytes 49152 | tf_op jit(solution)/shard_map/all_to_all | solution.py:120
  186.3 5.3 %all-to-all-done.4 = f32[16,1,384]{2,1,0:T(1,128)} async-done(((f32[16,1,384]{2,1,0:T(1,128)}), f32[16,1,384]{2,1,0:T(1,128)}, u32[]{:S(2)}, u32[]{:S(2)}) %all-to-all-start.4) | async-done | bytes 24608 | tf_op jit(solution)/shard_map/all_to_all | solution.py:120
  191.7 2.0 reduce.1
  193.7 2.1 reshape.168
  238.6 3.7 %all-to-all-start.5 = ((bf16[16,2,192]{2,1,0:T(2,128)(2,1)}), bf16[16,2,192]{2,1,0:T(2,128)(2,1)S(1)}, u32[]{:S(2)}, u32[]{:S(2)}) async-start(bf16[16,2,192]{2,1,0:T(2,128)(2,1)} %reshape.169), calls=%async_computation.5 | async-start | bytes 32768 | tf_op jit(solution)/shard_map/all_to_all | solution.py:126
  242.3 3.8 %convolution_bitcast_fusion = f32[384,384]{0,1:T(8,128)} fusion(bf16[2,1440,384]{2,1,0:T(8,128)(2,1)} %copy-done.1, bf16[2,1440,384]{2,1,0:T(8,128)(2,1)S(1)} %copy-done), kind=kOutput, calls=%fused_computation.56 | convolution fusion | flops 849346560 | bytes 5013504 | tf_op jit(solution)/shard_map/jkc,jkd->cd/dot_general | solution.py:156
  246.2 2.6 all-to-all-done.5
  259.7 4.1 %all-to-all-start.6 = ((bf16[16,2,192]{2,1,0:T(2,128)(2,1)}), bf16[16,2,192]{2,1,0:T(2,128)(2,1)}, u32[]{:S(2)}, u32[]{:S(2)}) async-start(bf16[16,2,192]{2,1,0:T(2,128)(2,1)} %reshape.171), calls=%async_computation.6 | async-start | bytes 32768 | tf_op jit(solution)/shard_map/all_to_all | solution.py:135
  263.9 2.5 fusion.41
  267.6 2.9 all-to-all-done.6
  272.7 3.5 %all-to-all-start.7 = ((bf16[16,2,192]{2,1,0:T(2,128)(2,1)}), bf16[16,2,192]{2,1,0:T(2,128)(2,1)S(1)}, u32[]{:S(2)}, u32[]{:S(2)}) async-start(bf16[16,2,192]{2,1,0:T(2,128)(2,1)} %reshape.173), calls=%async_computation.7 | async-start | bytes 32768 | tf_op jit(solution)/shard_map/all_to_all | solution.py:138
  278.7 3.9 %all-to-all-done.7 = bf16[16,2,192]{2,1,0:T(2,128)(2,1)S(1)} async-done(((bf16[16,2,192]{2,1,0:T(2,128)(2,1)}), bf16[16,2,192]{2,1,0:T(2,128)(2,1)S(1)}, u32[]{:S(2)}, u32[]{:S(2)}) %all-to-all-start.7) | async-done | bytes 12320 | tf_op jit(solution)/shard_map/all_to_all | solution.py:138
  285.2 3.9 %fusion.38 = bf16[2,1440,384]{2,1,0:T(8,128)(2,1)} fusion(bf16[2,1440,384]{2,1,0:T(8,128)(2,1)S(1)} %copy-done.6, f32[1440,2,384]{2,0,1:T(8,128)S(1)} %fusion.108, bf16[2,1440,384]{2,1,0:T(8,128)(2,1)S(1)} %copy-done.2, bf16[384,384]{1,0:T(8,128)(2,1)} %param.10), kind=kOutput, calls=%fused_computation.50 | convolution fusion | flops 853770240 | bytes 11354112 | tf_op jit(solution)/shard_map/jkd,cd->jkc/dot_general | solution.py:161
  289.1 50.2 %all-reduce.3.cloned.1.call-done = f32[384,384]{0,1:T(8,128)} async-done(((f32[384,384]{0,1:T(8,128)}), f32[384,384]{0,1:T(8,128)}) %all-reduce.3.cloned.1.call-update) | async-done | bytes 589840
  (364 shorter events, 162.4 us)
Async XLA Ops:
  7.2 1.7 copy-start
  7.2 11.1 %copy-start.13 = (f32[4]{0:T(128)S(1)}, f32[4]{0:T(128)}, u32[]{:S(2)}) copy-start(f32[4]{0:T(128)} %constant.106.clone) | copy-start | bytes 52
  7.2 11.0 %copy-start.14 = (s32[32]{0:T(128)S(1)}, s32[32]{0:T(128)}, u32[]{:S(2)}) copy-start(s32[32]{0:T(128)} %param.12) | copy-start | bytes 388
  7.4 0.6 copy-start.9
  7.4 167.3 %copy-start.7 = (bf16[1440,4]{0,1:T(4,128)(2,1)}, bf16[1440,4]{0,1:T(4,128)(2,1)S(1)}, u32[]{:S(2)}) copy-start(bf16[1440,4]{0,1:T(4,128)(2,1)S(1)} %get-tuple-element.365) | copy-start | bytes 34564
  10.6 55.4 %all-to-all-start = ((f32[16,1,384]{2,1,0:T(1,128)}), f32[16,1,384]{2,1,0:T(1,128)}, u32[]{:S(2)}, u32[]{:S(2)}) async-start(f32[16,1,384]{2,1,0:T(1,128)} %reshape.159), calls=%async_computation | async-start | bytes 49152 | tf_op jit(solution)/shard_map/all_to_all | solution.py:120
  66.0 63.9 %copy-start.3 = (bf16[2,2,384,384]{3,2,1,0:T(8,128)(2,1)S(1)}, bf16[2,2,384,384]{3,2,1,0:T(8,128)(2,1)}, u32[]{:S(2)}) copy-start(bf16[2,2,384,384]{3,2,1,0:T(8,128)(2,1)} %param.11) | copy-start | bytes 3538948
  168.6 1.7 copy-start.5
  168.6 1.7 copy-start.12
  170.3 5.8 %copy-start.10 = (bf16[1440,4]{0,1:T(4,128)(2,1)S(1)}, bf16[1440,4]{0,1:T(4,128)(2,1)}, u32[]{:S(2)}) copy-start(bf16[1440,4]{0,1:T(4,128)(2,1)} %copy-done.9) | copy-start | bytes 34564
  174.7 1.4 copy-start.1
  176.1 9.0 %copy-start.15 = (u32[32]{0:T(128)S(1)}, u32[32]{0:T(128)}, u32[]{:S(2)}) copy-start(u32[32]{0:T(128)} %constant.112) | copy-start | bytes 388
  180.9 10.7 %all-to-all-start.4 = ((f32[16,1,384]{2,1,0:T(1,128)}), f32[16,1,384]{2,1,0:T(1,128)}, u32[]{:S(2)}, u32[]{:S(2)}) async-start(f32[16,1,384]{2,1,0:T(1,128)} %reshape.167), calls=%async_computation.4 | async-start | bytes 49152 | tf_op jit(solution)/shard_map/all_to_all | solution.py:120
  238.6 10.1 %all-to-all-start.5 = ((bf16[16,2,192]{2,1,0:T(2,128)(2,1)}), bf16[16,2,192]{2,1,0:T(2,128)(2,1)S(1)}, u32[]{:S(2)}, u32[]{:S(2)}) async-start(bf16[16,2,192]{2,1,0:T(2,128)(2,1)} %reshape.169), calls=%async_computation.5 | async-start | bytes 32768 | tf_op jit(solution)/shard_map/all_to_all | solution.py:126
  242.3 97.1 %all-reduce.3.cloned.1.call-start = ((), (), s32[]{:S(2)}) async-start(), calls=%async_computation.8 | async-start | bytes 1179648
  255.8 10.6 %copy-start.4 = (f32[2,384,384]{2,1,0:T(8,128)S(1)}, f32[2,384,384]{2,1,0:T(8,128)}, u32[]{:S(2)}) copy-start(f32[2,384,384]{2,1,0:T(8,128)} %fusion.92) | copy-start | bytes 3538948
  259.7 10.7 %all-to-all-start.6 = ((bf16[16,2,192]{2,1,0:T(2,128)(2,1)}), bf16[16,2,192]{2,1,0:T(2,128)(2,1)}, u32[]{:S(2)}, u32[]{:S(2)}) async-start(bf16[16,2,192]{2,1,0:T(2,128)(2,1)} %reshape.171), calls=%async_computation.6 | async-start | bytes 32768 | tf_op jit(solution)/shard_map/all_to_all | solution.py:135
  272.7 10.0 %all-to-all-start.7 = ((bf16[16,2,192]{2,1,0:T(2,128)(2,1)}), bf16[16,2,192]{2,1,0:T(2,128)(2,1)S(1)}, u32[]{:S(2)}, u32[]{:S(2)}) async-start(bf16[16,2,192]{2,1,0:T(2,128)(2,1)} %reshape.173), calls=%async_computation.7 | async-start | bytes 32768 | tf_op jit(solution)/shard_map/all_to_all | solution.py:138
  276.2 6.7 %copy-start.8 = (bf16[1440,4]{0,1:T(4,128)(2,1)S(1)}, bf16[1440,4]{0,1:T(4,128)(2,1)}, u32[]{:S(2)}) copy-start(bf16[1440,4]{0,1:T(4,128)(2,1)} %copy-done.7) | copy-start | bytes 34564
  276.2 6.7 %copy-start.11 = (bf16[1440,4]{0,1:T(4,128)(2,1)S(1)}, bf16[1440,4]{0,1:T(4,128)(2,1)}, u32[]{:S(2)}) copy-start(bf16[1440,4]{0,1:T(4,128)(2,1)} %copy-done.9) | copy-start | bytes 34564
  282.9 1.6 copy-start.2
  282.9 2.3 copy-start.6
Sparse Core Ops, SparseCore 0:
  246.5 92.8 all-reduce.2
